TPU v7x, 256 devices: a whole 4x4x8 slice. The times are simulated.
256 devices in a mesh: seq: 8 (over z_hi, core), chan: 16 (over y, x), dp: 2 (over z_lo).
Axes of the slice: x: 4, y: 4, z: 8 (z_hi: 4, z_lo: 2; z = z_hi * 2 + z_lo), core: 2. Of those that a mesh axis runs over, the one named last changes fastest.
Arguments:
- query_proj: bfloat16 [2, 4096, 8192], P('dp', 'seq', 'chan'), may hold values from -6 to 6
- key_proj: bfloat16 [2, 4096, 8192], P('dp', 'seq', 'chan')
- value_proj: bfloat16 [2, 4096, 8192], P('dp', 'seq', 'chan')
- cotangent: bfloat16 [2, 4096, 8192], P('dp', 'seq', 'chan'), may hold values from -6 to 6
- long_filter: float32 [4096, 8192], P('seq', 'chan')
- skip_gain: float32 [8192], P('chan'), may hold values from -3 to 3
Outputs:
- output: bfloat16 [2, 4096, 8192], P('dp', 'seq', 'chan')
- grad_query: bfloat16 [2, 4096, 8192], P('dp', 'seq', 'chan')
- grad_key: bfloat16 [2, 4096, 8192], P('dp', 'seq', 'chan')
- grad_value: bfloat16 [2, 4096, 8192], P('dp', 'seq', 'chan')
- grad_filter: float32 [4096, 8192], P('seq', 'chan')
- grad_skip: float32 [8192], P('chan')
All inputs are finite; a program needn't handle non-finite values.
Results may differ from a plain program's by a relative error of at most 0.0095.
Values may be sent and summed in bfloat16 or wider, within the bound.
No kernel may reach another device: no remote copies, remote signals or barrier semaphores. Data moves between devices by JAX's collectives and lax.ppermute only.
A program may use at most 64 MiB of HBM per device.

v0:
```python
import math
import jax
import jax.numpy as jnp
from jax import lax
from jax.sharding import PartitionSpec as P

full_precision = lax.Precision.HIGHEST


def dft_tables(seq_length):
    full_size = 2 * seq_length
    inner_size = 128
    outer_size = full_size // inner_size
    half_size = outer_size // 2
    outer_index = jnp.arange(outer_size, dtype=jnp.int32)
    half_index = jnp.arange(half_size, dtype=jnp.int32)
    inner_index = jnp.arange(inner_size, dtype=jnp.int32)
    first_angle = (
        2.0
        * math.pi
        / outer_size
        * (outer_index[:, None] * half_index[None, :] % outer_size).astype(jnp.float32)
    )
    twist_angle = (
        2.0
        * math.pi
        / full_size
        * (outer_index[:, None] * inner_index[None, :] % full_size).astype(jnp.float32)
    )
    last_angle = (
        2.0
        * math.pi
        / inner_size
        * (inner_index[:, None] * inner_index[None, :] % inner_size).astype(jnp.float32)
    )
    return (
        jnp.cos(first_angle),
        jnp.sin(first_angle),
        jnp.cos(twist_angle),
        jnp.sin(twist_angle),
        jnp.cos(last_angle),
        jnp.sin(last_angle),
    )


def forward(signal, tables):
    cos_first, sin_first, cos_twist, sin_twist, cos_last, sin_last = tables
    half_size = cos_first.shape[1]
    signal_grid = signal.reshape(signal.shape[0], half_size, 128)
    real_first = jnp.einsum("kn,rnm->rkm", cos_first, signal_grid, precision=full_precision)
    imag_first = -jnp.einsum("kn,rnm->rkm", sin_first, signal_grid, precision=full_precision)
    real_twist = real_first * cos_twist + imag_first * sin_twist
    imag_twist = imag_first * cos_twist - real_first * sin_twist
    real_last = jnp.einsum(
        "rkm,mj->rkj", real_twist, cos_last, precision=full_precision
    ) + jnp.einsum("rkm,mj->rkj", imag_twist, sin_last, precision=full_precision)
    imag_last = jnp.einsum(
        "rkm,mj->rkj", imag_twist, cos_last, precision=full_precision
    ) - jnp.einsum("rkm,mj->rkj", real_twist, sin_last, precision=full_precision)
    return (real_last, imag_last)


def inverse(real_part, imag_part, tables):
    cos_first, sin_first, cos_twist, sin_twist, cos_last, sin_last = tables
    half_size = cos_first.shape[1]
    row_total = real_part.shape[0]
    real_inner = jnp.einsum(
        "rkj,jm->rkm", real_part, cos_last, precision=full_precision
    ) - jnp.einsum("rkj,jm->rkm", imag_part, sin_last, precision=full_precision)
    imag_inner = jnp.einsum(
        "rkj,jm->rkm", imag_part, cos_last, precision=full_precision
    ) + jnp.einsum("rkj,jm->rkm", real_part, sin_last, precision=full_precision)
    real_twist = real_inner * cos_twist - imag_inner * sin_twist
    imag_twist = imag_inner * cos_twist + real_inner * sin_twist
    result = jnp.einsum(
        "kn,rkm->rnm", cos_first, real_twist, precision=full_precision
    ) - jnp.einsum("kn,rkm->rnm", sin_first, imag_twist, precision=full_precision)
    return (result / (2.0 * half_size * 128)).reshape(row_total, half_size * 128)


def filter_block(items, tables):
    mixed_blk, weighted_blk, kernel = items
    batches, chan_width, seq_length = mixed_blk.shape
    row_count = batches * chan_width
    mixed_wide = mixed_blk.astype(jnp.float32)
    weighted_wide = weighted_blk.astype(jnp.float32)
    stacked = jnp.concatenate(
        [
            mixed_wide.reshape(row_count, seq_length),
            weighted_wide.reshape(row_count, seq_length),
            kernel,
        ],
        axis=0,
    )
    real_spec, imag_spec = forward(stacked, tables)
    grid_shape = real_spec.shape[1:]
    mixed_real = real_spec[:row_count].reshape((batches, chan_width) + grid_shape)
    mixed_imag = imag_spec[:row_count].reshape((batches, chan_width) + grid_shape)
    weighted_real = real_spec[row_count : 2 * row_count].reshape((batches, chan_width) + grid_shape)
    weighted_imag = imag_spec[row_count : 2 * row_count].reshape((batches, chan_width) + grid_shape)
    kernel_real = real_spec[2 * row_count :][None]
    kernel_imag = imag_spec[2 * row_count :][None]
    conv_real = mixed_real * kernel_real - mixed_imag * kernel_imag
    conv_imag = mixed_real * kernel_imag + mixed_imag * kernel_real
    corr_real = kernel_real * weighted_real + kernel_imag * weighted_imag
    corr_imag = kernel_real * weighted_imag - kernel_imag * weighted_real
    slope_real = jnp.sum(mixed_real * weighted_real + mixed_imag * weighted_imag, axis=0)
    slope_imag = jnp.sum(mixed_real * weighted_imag - mixed_imag * weighted_real, axis=0)
    spec_real = jnp.concatenate(
        [
            conv_real.reshape((row_count,) + grid_shape),
            corr_real.reshape((row_count,) + grid_shape),
            slope_real,
        ],
        axis=0,
    )
    spec_imag = jnp.concatenate(
        [
            conv_imag.reshape((row_count,) + grid_shape),
            corr_imag.reshape((row_count,) + grid_shape),
            slope_imag,
        ],
        axis=0,
    )
    result = inverse(spec_real, spec_imag, tables)
    conv_vals = result[:row_count].reshape(batches, chan_width, seq_length).astype(jnp.bfloat16)
    corr_vals = (
        result[row_count : 2 * row_count]
        .reshape(batches, chan_width, seq_length)
        .astype(jnp.bfloat16)
    )
    slope = result[2 * row_count :]
    return (conv_vals, corr_vals, slope)


def run_blocks(mixed_rows, weighted_rows, filter_part):
    batches, part_width, seq_length = mixed_rows.shape
    block_width = min(part_width, 8)
    block_count = part_width // block_width
    tables = dft_tables(seq_length)

    def stack_rows(arr):
        return jnp.moveaxis(arr.reshape(batches, block_count, block_width, seq_length), 1, 0)

    def unstack_rows(arr):
        return jnp.moveaxis(arr, 0, 1).reshape(batches, part_width, seq_length)

    def one_block(items):
        return filter_block(items, tables)

    items = (
        stack_rows(mixed_rows),
        stack_rows(weighted_rows),
        filter_part.reshape(block_count, block_width, seq_length),
    )
    conv_vals, corr_vals, slope = lax.map(one_block, items)
    return (unstack_rows(conv_vals), unstack_rows(corr_vals), slope.reshape(part_width, seq_length))


def on_device(query_proj, key_proj, value_proj, cotangent, long_filter, skip_gain):
    query_rows = query_proj[0].astype(jnp.float32)
    key_rows = key_proj[0].astype(jnp.float32)
    value_rows = value_proj[0].astype(jnp.float32)
    cot_rows = cotangent[0].astype(jnp.float32)
    local_length = query_proj.shape[1]
    chan_width = query_proj.shape[2]
    seq_count = lax.axis_size("seq")
    batch_count = lax.axis_size("dp")
    factor = (batch_count * seq_count * local_length) ** (-0.5)
    mixed = (key_rows * value_rows).astype(jnp.bfloat16)
    weighted = (cot_rows * query_rows).astype(jnp.bfloat16)
    mixed_wide = mixed.astype(jnp.float32)
    weighted_wide = weighted.astype(jnp.float32)
    gain_term = factor * jnp.sum(weighted_wide * mixed_wide, axis=0)
    grad_skip = lax.psum(gain_term, ("seq", "dp"))
    filter_share = lax.all_to_all(long_filter.T, "seq", split_axis=0, concat_axis=1, tiled=True)
    groups = seq_count * batch_count
    share_width = chan_width // groups
    mixed_cols, weighted_cols = (
        lax.all_to_all(mixed.T, ("seq", "dp"), split_axis=0, concat_axis=1, tiled=True),
        lax.all_to_all(weighted.T, ("seq", "dp"), split_axis=0, concat_axis=1, tiled=True),
    )

    def to_sequences(arr):
        arr = arr.reshape(share_width, seq_count, batch_count, local_length)
        return jnp.transpose(arr, (2, 0, 1, 3)).reshape(
            batch_count, share_width, seq_count * local_length
        )

    def to_pieces(arr):
        arr = arr.reshape(batch_count, share_width, seq_count, local_length)
        return jnp.transpose(arr, (1, 2, 0, 3)).reshape(share_width, groups * local_length)

    filter_part = lax.dynamic_slice_in_dim(
        filter_share, lax.axis_index("dp") * share_width, share_width, 0
    )
    conv_vals, corr_vals, slope = run_blocks(
        to_sequences(mixed_cols), to_sequences(weighted_cols), filter_part
    )
    conv_back, corr_back = (
        lax.all_to_all(
            to_pieces(conv_vals), ("seq", "dp"), split_axis=1, concat_axis=0, tiled=True
        ),
        lax.all_to_all(
            to_pieces(corr_vals), ("seq", "dp"), split_axis=1, concat_axis=0, tiled=True
        ),
    )
    slope_share = lax.all_gather(slope, "dp", axis=0, tiled=True)
    slope_rows = lax.all_to_all(slope_share, "seq", split_axis=1, concat_axis=0, tiled=True)
    grad_filter = factor * slope_rows.T
    conv_rows = conv_back.T.astype(jnp.float32)
    corr_rows = corr_back.T.astype(jnp.float32)
    signal = conv_rows + skip_gain[None, :] * mixed_wide
    output = (query_rows * signal).astype(jnp.bfloat16)
    grad_query = (cot_rows * signal).astype(jnp.bfloat16)
    back = corr_rows + skip_gain[None, :] * weighted_wide
    grad_key = (back * value_rows).astype(jnp.bfloat16)
    grad_value = (back * key_rows).astype(jnp.bfloat16)
    return (
        output[None],
        grad_query[None],
        grad_key[None],
        grad_value[None],
        grad_filter,
        grad_skip,
    )


def solution(mesh):
    return jax.shard_map(
        on_device,
        mesh=mesh,
        in_specs=(
            P("dp", "seq", "chan"),
            P("dp", "seq", "chan"),
            P("dp", "seq", "chan"),
            P("dp", "seq", "chan"),
            P("seq", "chan"),
            P("chan"),
        ),
        out_specs=(
            P("dp", "seq", "chan"),
            P("dp", "seq", "chan"),
            P("dp", "seq", "chan"),
            P("dp", "seq", "chan"),
            P("seq", "chan"),
            P("chan"),
        ),
        check_vma=False,
    )
```

profile of v0, /device:TPU:32, one launch (start us, length us, event | category | flops | bytes accessed | tf_op | source)
XLA Modules:
  0.0 319.2 jit_solution(15264044031151015225)
XLA Ops:
  11.3 22.9 %all_to_all.90 = bf16[16,32,512]{2,1,0:T(8,128)(2,1)S(1)} all-to-all(bf16[16,32,512]{2,1,0:T(8,128)(2,1)S(1)} %bitcast.249), channel_id=1, replica_groups=mesh['seq'=8,'chan'=16,'dp'=2] {'seq','dp'}, dimensions={0} | all-to-all | bytes 1048576 | tf_op jit(solution)/shard_map/all_to_all | solution.py:181
  34.1 5.7 %all-to-all-start = ((bf16[16,32,512]{2,1,0:T(8,128)(2,1)}), bf16[16,32,512]{2,1,0:T(8,128)(2,1)S(1)}, u32[]{:S(2)}, u32[]{:S(2)}) async-start(bf16[16,32,512]{2,1,0:T(8,128)(2,1)} %bitcast.4), calls=%async_computation | async-start | bytes 1048576 | tf_op jit(solution)/shard_map/all_to_all | solution.py:180
  41.2 13.2 %all-to-all-done = bf16[16,32,512]{2,1,0:T(8,128)(2,1)S(1)} async-done(((bf16[16,32,512]{2,1,0:T(8,128)(2,1)}), bf16[16,32,512]{2,1,0:T(8,128)(2,1)S(1)}, u32[]{:S(2)}, u32[]{:S(2)}) %all-to-all-start) | async-done | bytes 524320 | tf_op jit(solution)/shard_map/all_to_all | solution.py:180
  54.4 4.8 %all-to-all-start.2 = ((f32[8,64,512]{2,1,0:T(8,128)}), f32[8,64,512]{2,1,0:T(8,128)S(1)}, u32[]{:S(2)}, u32[]{:S(2)}) async-start(f32[8,64,512]{2,1,0:T(8,128)} %bitcast.18), calls=%async_computation.2 | async-start | bytes 2097152 | tf_op jit(solution)/shard_map/all_to_all | solution.py:176
  61.9 26.4 %all-to-all-done.2 = f32[8,64,512]{2,1,0:T(8,128)S(1)} async-done(((f32[8,64,512]{2,1,0:T(8,128)}), f32[8,64,512]{2,1,0:T(8,128)S(1)}, u32[]{:S(2)}, u32[]{:S(2)}) %all-to-all-start.2) | async-done | bytes 1048608 | tf_op jit(solution)/shard_map/all_to_all | solution.py:176
  89.3 108.2 %while.16 = (s32[]{:T(128)}, bf16[4,2,8,4096]{3,2,1,0:T(8,128)(2,1)}, bf16[4,2,8,4096]{3,2,1,0:T(8,128)(2,1)}, f32[4,8,4096]{2,1,0:T(8,128)}, bf16[4,2,8,4096]{3...) while((s32[]{:T(128)}, ...), condition=%wide.region_3.4_spmd.clone.clone, body=%wide.region_0.3_spmd.clone.clone.sunk | while | flops 4545183744 | bytes 59639460 | solution.py:156
  102.2 2.4 fusion.201
  104.6 1.8 reduce_sum.35
  106.4 2.5 convolution_add_fusion.5
  129.3 2.4 fusion.201
  133.5 2.5 convolution_add_fusion.5
  156.3 2.4 fusion.201
  160.5 2.5 convolution_add_fusion.5
  183.3 2.4 fusion.201
  187.6 2.5 convolution_add_fusion.5
  199.7 4.5 %all-to-all-start.3 = ((bf16[32,16,512]{2,0,1:T(8,128)(2,1)}), bf16[32,16,512]{2,0,1:T(8,128)(2,1)S(1)}, u32[]{:S(2)}, u32[]{:S(2)}) async-start(bf16[32,16,512]{2,0,1:T(8,128)(2,1)} %bitcast.23), calls=%async_computation.3 | async-start | bytes 1048576 | tf_op jit(solution)/shard_map/all_to_all | solution.py:201
  205.9 12.8 %all-to-all-done.3 = bf16[32,16,512]{2,0,1:T(8,128)(2,1)S(1)} async-done(((bf16[32,16,512]{2,0,1:T(8,128)(2,1)}), bf16[32,16,512]{2,0,1:T(8,128)(2,1)S(1)}, u32[]{:S(2)}, u32[]{:S(2)}) %all-to-all-start.3) | async-done | bytes 524320 | tf_op jit(solution)/shard_map/all_to_all | solution.py:201
  218.7 5.8 %all-to-all-start.4 = ((bf16[32,16,512]{2,0,1:T(8,128)(2,1)}), bf16[32,16,512]{2,0,1:T(8,128)(2,1)}, u32[]{:S(2)}, u32[]{:S(2)}) async-start(bf16[32,16,512]{2,0,1:T(8,128)(2,1)} %bitcast.32), calls=%async_computation.4 | async-start | bytes 1048576 | tf_op jit(solution)/shard_map/all_to_all | solution.py:204
  224.5 19.5 %all-gather.2.cloned.1.call-done = f32[64,4096]{1,0:T(8,128)} async-done(((f32[32,4096]{1,0:T(8,128)}), f32[64,4096]{1,0:T(8,128)}) %all-gather.2.cloned.1.call-update) | async-done | bytes 1048592 | tf_op jit(solution)/shard_map/all_gather | solution.py:208
  244.0 2.3 copy.83
  246.4 7.9 %all-to-all-start.5 = ((f32[64,8,512]{2,0,1:T(8,128)}), f32[64,8,512]{2,0,1:T(8,128)}, u32[]{:S(2)}, u32[]{:S(2)}) async-start(f32[64,8,512]{2,0,1:T(8,128)} %bitcast.251), calls=%async_computation.5 | async-start | bytes 2097152 | tf_op jit(solution)/shard_map/all_to_all | solution.py:209
  254.3 47.0 %psum.7 = f32[512]{0:T(512)} all-reduce(f32[512]{0:T(512)S(1)} %broadcast_multiply_fusion.1), channel_id=1, replica_groups=mesh['seq'=8,'chan'=16,'dp'=2] {'seq','dp'}, use_global_device_ids=true, to_apply=%region_5.6 | all-reduce | flops 512 | bytes 4096 | tf_op jit(solution)/shard_map/psum | solution.py:175
  301.3 3.2 %fusion.150 = (bf16[512,512]{0,1:T(8,128)(2,1)}, bf16[512,512]{0,1:T(8,128)(2,1)}, bf16[512,512]{0,1:T(8,128)(2,1)}, bf16[512,512]{0,1:T(8,128)(2,1)}) fusion(bf16[512,512]{0,1:T(8,128)(2,1)S(1)} %copy-done.11, bf16[32,16,512]{2,0,1:T(8,128)(2,1)} %all-to-all-done.4, bf16[1,512,512]{1,2,0:T(8,128)(2,1)S(1)} %copy-done.5, f32[512]{0:T(512)S(1)} %copy-done.20, ...), kind=kLoop, calls=%fused_computation.173 | loop fusion | flops 5242880 | bytes 6293504 | tf_op jit(solution)/shard_map/convert_element_type | solution.py:218
  304.6 2.1 copy.65
  (210 shorter events, 104.6 us)
Async XLA Ops:
  7.2 1.6 copy-start.17
  7.2 1.9 copy-start.18
  8.8 1.7 copy-start.4
  10.5 29.4 %copy-start.15 = (f32[512,512]{1,0:T(8,128)S(1)}, f32[512,512]{1,0:T(8,128)}, u32[]{:S(2)}) copy-start(f32[512,512]{1,0:T(8,128)} %param.12) | copy-start | bytes 3145732
  34.1 20.2 %all-to-all-start = ((bf16[16,32,512]{2,1,0:T(8,128)(2,1)}), bf16[16,32,512]{2,1,0:T(8,128)(2,1)S(1)}, u32[]{:S(2)}, u32[]{:S(2)}) async-start(bf16[16,32,512]{2,1,0:T(8,128)(2,1)} %bitcast.4), calls=%async_computation | async-start | bytes 1048576 | tf_op jit(solution)/shard_map/all_to_all | solution.py:180
  54.4 34.0 %all-to-all-start.2 = ((f32[8,64,512]{2,1,0:T(8,128)}), f32[8,64,512]{2,1,0:T(8,128)S(1)}, u32[]{:S(2)}, u32[]{:S(2)}) async-start(f32[8,64,512]{2,1,0:T(8,128)} %bitcast.18), calls=%async_computation.2 | async-start | bytes 2097152 | tf_op jit(solution)/shard_map/all_to_all | solution.py:176
  106.4 2.5 copy-start.1
  133.5 2.5 copy-start.1
  160.5 2.5 copy-start.1
  187.5 2.5 copy-start.1
  198.8 5.5 %copy-start.19 = (bf16[4,2,8,4096]{3,2,1,0:T(8,128)(2,1)S(1)}, bf16[4,2,8,4096]{3,2,1,0:T(8,128)(2,1)}, u32[]{:S(2)}) copy-start(bf16[4,2,8,4096]{3,2,1,0:T(8,128)(2,1)} %get-tuple-element.118) | copy-start | bytes 1572868
  199.7 19.0 %all-to-all-start.3 = ((bf16[32,16,512]{2,0,1:T(8,128)(2,1)}), bf16[32,16,512]{2,0,1:T(8,128)(2,1)S(1)}, u32[]{:S(2)}, u32[]{:S(2)}) async-start(bf16[32,16,512]{2,0,1:T(8,128)(2,1)} %bitcast.23), calls=%async_computation.3 | async-start | bytes 1048576 | tf_op jit(solution)/shard_map/all_to_all | solution.py:201
  204.2 39.8 %all-gather.2.cloned.1.call-start = ((), (), s32[]{:S(2)}) async-start(), calls=%async_computation.6 | async-start | bytes 1572864 | tf_op jit(solution)/shard_map/all_gather | solution.py:208
  218.7 27.7 %all-to-all-start.4 = ((bf16[32,16,512]{2,0,1:T(8,128)(2,1)}), bf16[32,16,512]{2,0,1:T(8,128)(2,1)}, u32[]{:S(2)}, u32[]{:S(2)}) async-start(bf16[32,16,512]{2,0,1:T(8,128)(2,1)} %bitcast.32), calls=%async_computation.4 | async-start | bytes 1048576 | tf_op jit(solution)/shard_map/all_to_all | solution.py:204
  244.0 57.3 %copy-start.11 = (bf16[512,512]{0,1:T(8,128)(2,1)S(1)}, bf16[512,512]{0,1:T(8,128)(2,1)}, u32[]{:S(2)}) copy-start(bf16[512,512]{0,1:T(8,128)(2,1)} %copy-done.10) | copy-start | bytes 1572868
  246.3 55.0 %copy-start.3 = (bf16[1,512,512]{1,2,0:T(8,128)(2,1)S(1)}, bf16[1,512,512]{1,2,0:T(8,128)(2,1)}, u32[]{:S(2)}) copy-start(bf16[1,512,512]{1,2,0:T(8,128)(2,1)} %copy-done.2) | copy-start | bytes 1572868
  246.3 55.0 %copy-start.5 = (bf16[1,512,512]{1,2,0:T(8,128)(2,1)S(1)}, bf16[1,512,512]{1,2,0:T(8,128)(2,1)}, u32[]{:S(2)}) copy-start(bf16[1,512,512]{1,2,0:T(8,128)(2,1)} %copy-done.4) | copy-start | bytes 1572868
  246.4 55.0 %copy-start.7 = (bf16[1,512,512]{1,2,0:T(8,128)(2,1)S(1)}, bf16[1,512,512]{1,2,0:T(8,128)(2,1)}, u32[]{:S(2)}) copy-start(bf16[1,512,512]{1,2,0:T(8,128)(2,1)} %copy-done.6) | copy-start | bytes 1572868
  246.4 55.0 %copy-start.9 = (bf16[1,512,512]{1,2,0:T(8,128)(2,1)S(1)}, bf16[1,512,512]{1,2,0:T(8,128)(2,1)}, u32[]{:S(2)}) copy-start(bf16[1,512,512]{1,2,0:T(8,128)(2,1)} %copy-done.8) | copy-start | bytes 1572868
  246.4 55.0 %copy-start.20 = (f32[512]{0:T(512)S(1)}, f32[512]{0:T(512)}, u32[]{:S(2)}) copy-start(f32[512]{0:T(512)} %param.13) | copy-start | bytes 6148
  246.4 63.3 %all-to-all-start.5 = ((f32[64,8,512]{2,0,1:T(8,128)}), f32[64,8,512]{2,0,1:T(8,128)}, u32[]{:S(2)}, u32[]{:S(2)}) async-start(f32[64,8,512]{2,0,1:T(8,128)} %bitcast.251), calls=%async_computation.5 | async-start | bytes 2097152 | tf_op jit(solution)/shard_map/all_to_all | solution.py:209
  304.6 2.1 copy-start.14
  304.6 3.1 copy-start.13
  306.7 2.0 copy-start.12
  (9 other events, 11.4 us)
Sparse Core Ops, SparseCore 0:
  206.8 37.1 all-gather.1
where the time goes:
time: 321 us; the launch traced here: 319 us
  matrix products  74.1 us (23%)
  waiting for transfers between devices  72.4 us (23%)
  blocking collectives  69.9 us (22%)
  local copies, waits for them, and re-layouts  33.4 us (10%)
  starting transfers between devices  28.7 us (9%)
  other arithmetic  25.6 us (8%)
  between operations  14.3 us (4%)
    psum x1, blocking collectives, on_device(): grad_skip = lax.psum(gain_term, ('seq', 'dp'))  47 us
    all_to_all x1, waiting for transfers between devices, on_device(): lax.all_to_all(long_filter.T, 'seq', split_axis=0, concat_axis=1, tiled=T...  26.4 us
    all_to_all x1, blocking collectives, on_device(): lax.all_to_all(weighted.T, ('seq', 'dp'), split_axis=0, concat_axis=1, ti...  22.9 us
    all_gather x1, waiting for transfers between devices, on_device(): slope_share = lax.all_gather(slope, 'dp', axis=0, tiled=True)  19.5 us
    all_to_all x1, waiting for transfers between devices, on_device(): lax.all_to_all(mixed.T, ('seq', 'dp'), split_axis=0, concat_axis=1, tiled...  13.2 us
    all_to_all x1, waiting for transfers between devices, on_device(): lax.all_to_all(to_pieces(conv_vals), ('seq', 'dp'), split_axis=1, concat_...  12.8 us
    unnamed x50, local copies, waits for them, and re-layouts  11.1 us
    dot_general x4, matrix products, inverse(): jnp.einsum('rkj,jm->rkm', real_part, sin_last, precision=full_precision)  9.98 us
  transfers between devices with their start and end apart: 6, of which 4 were waited for; matrix products, arithmetic and copies ran while one was open for 5% of the time, Pallas kernels for 0%

commit v1 on v0

--- a/solution.py
+++ b/solution.py
@@ -5,6 +5,12 @@
 from jax.sharding import PartitionSpec as P
 
 full_precision = lax.Precision.HIGHEST
+
+
+def _measure_turns(block_here, which_axis, bus_axis):
+    for i in (which_axis, bus_axis):
+        block_here = lax.psum(block_here, axis_name=i)
+    return block_here
 
 
 def dft_tables(seq_length):
@@ -172,7 +178,7 @@
     mixed_wide = mixed.astype(jnp.float32)
     weighted_wide = weighted.astype(jnp.float32)
     gain_term = factor * jnp.sum(weighted_wide * mixed_wide, axis=0)
-    grad_skip = lax.psum(gain_term, ("seq", "dp"))
+    grad_skip = _measure_turns(gain_term, which_axis="seq", bus_axis="dp")
     filter_share = lax.all_to_all(long_filter.T, "seq", split_axis=0, concat_axis=1, tiled=True)
     groups = seq_count * batch_count
     share_width = chan_width // groups

time: 321 us -> 315 us (0.981)
  blocking collectives: 69.9 us -> 64 us
    psum x1 -> x2, blocking collectives: 47 us -> 41.2 us  [_measure_turns(): block_here = lax.psum(block_here, axis_name=i)]
where the time goes in v1:
time: 315 us; the launch traced here: 313 us
  matrix products  74.1 us (24%)
  waiting for transfers between devices  72.4 us (23%)
  blocking collectives  64 us (20%)
  local copies, waits for them, and re-layouts  33.4 us (11%)
  starting transfers between devices  28.7 us (9%)
  other arithmetic  25.4 us (8%)
  between operations  14.3 us (5%)
    psum x2, blocking collectives, _measure_turns(): block_here = lax.psum(block_here, axis_name=i)  41.2 us
    all_to_all x1, waiting for transfers between devices, on_device(): lax.all_to_all(long_filter.T, 'seq', split_axis=0, concat_axis=1, tiled=T...  26.4 us
    all_to_all x1, blocking collectives, on_device(): lax.all_to_all(weighted.T, ('seq', 'dp'), split_axis=0, concat_axis=1, ti...  22.9 us
    all_gather x1, waiting for transfers between devices, on_device(): slope_share = lax.all_gather(slope, 'dp', axis=0, tiled=True)  19.5 us
    all_to_all x1, waiting for transfers between devices, on_device(): lax.all_to_all(mixed.T, ('seq', 'dp'), split_axis=0, concat_axis=1, tiled...  13.2 us
    all_to_all x1, waiting for transfers between devices, on_device(): lax.all_to_all(to_pieces(conv_vals), ('seq', 'dp'), split_axis=1, concat_...  12.8 us
    unnamed x50, local copies, waits for them, and re-layouts  11.1 us
    dot_general x4, matrix products, inverse(): jnp.einsum('rkj,jm->rkm', real_part, sin_last, precision=full_precision)  10 us
  transfers between devices with their start and end apart: 6, of which 4 were waited for; matrix products, arithmetic and copies ran while one was open for 5% of the time, Pallas kernels for 0%

profile of v1, /device:TPU:32, one launch (start us, length us, event | category | flops | bytes accessed | tf_op | source)
XLA Modules:
  0.0 313.2 jit_solution(14485106665526045109)
XLA Ops:
  11.3 22.9 %all_to_all.90 = bf16[16,32,512]{2,1,0:T(8,128)(2,1)S(1)} all-to-all(bf16[16,32,512]{2,1,0:T(8,128)(2,1)S(1)} %bitcast.249), channel_id=1, replica_groups=mesh['seq'=8,'chan'=16,'dp'=2] {'seq','dp'}, dimensions={0} | all-to-all | bytes 1048576 | tf_op jit(solution)/shard_map/all_to_all | solution.py:187
  34.1 5.7 %all-to-all-start = ((bf16[16,32,512]{2,1,0:T(8,128)(2,1)}), bf16[16,32,512]{2,1,0:T(8,128)(2,1)S(1)}, u32[]{:S(2)}, u32[]{:S(2)}) async-start(bf16[16,32,512]{2,1,0:T(8,128)(2,1)} %bitcast.4), calls=%async_computation | async-start | bytes 1048576 | tf_op jit(solution)/shard_map/all_to_all | solution.py:186
  41.2 13.2 %all-to-all-done = bf16[16,32,512]{2,1,0:T(8,128)(2,1)S(1)} async-done(((bf16[16,32,512]{2,1,0:T(8,128)(2,1)}), bf16[16,32,512]{2,1,0:T(8,128)(2,1)S(1)}, u32[]{:S(2)}, u32[]{:S(2)}) %all-to-all-start) | async-done | bytes 524320 | tf_op jit(solution)/shard_map/all_to_all | solution.py:186
  54.4 4.8 %all-to-all-start.2 = ((f32[8,64,512]{2,1,0:T(8,128)}), f32[8,64,512]{2,1,0:T(8,128)S(1)}, u32[]{:S(2)}, u32[]{:S(2)}) async-start(f32[8,64,512]{2,1,0:T(8,128)} %bitcast.18), calls=%async_computation.2 | async-start | bytes 2097152 | tf_op jit(solution)/shard_map/all_to_all | solution.py:182
  61.9 26.4 %all-to-all-done.2 = f32[8,64,512]{2,1,0:T(8,128)S(1)} async-done(((f32[8,64,512]{2,1,0:T(8,128)}), f32[8,64,512]{2,1,0:T(8,128)S(1)}, u32[]{:S(2)}, u32[]{:S(2)}) %all-to-all-start.2) | async-done | bytes 1048608 | tf_op jit(solution)/shard_map/all_to_all | solution.py:182
  89.3 108.0 %while.16 = (s32[]{:T(128)}, bf16[4,2,8,4096]{3,2,1,0:T(8,128)(2,1)}, bf16[4,2,8,4096]{3,2,1,0:T(8,128)(2,1)}, f32[4,8,4096]{2,1,0:T(8,128)}, bf16[4,2,8,4096]{3...) while((s32[]{:T(128)}, ...), condition=%wide.region_3.4_spmd.clone.clone, body=%wide.region_0.3_spmd.clone.clone.sunk | while | flops 4545183744 | bytes 59639460 | solution.py:162
  102.2 2.4 fusion.201
  106.4 2.5 convolution_add_fusion.5
  129.2 2.4 fusion.201
  133.4 2.5 convolution_add_fusion.5
  156.2 2.4 fusion.201
  160.4 2.5 convolution_add_fusion.5
  183.2 2.4 fusion.201
  187.4 2.5 convolution_add_fusion.5
  199.5 4.5 %all-to-all-start.3 = ((bf16[32,16,512]{2,0,1:T(8,128)(2,1)}), bf16[32,16,512]{2,0,1:T(8,128)(2,1)S(1)}, u32[]{:S(2)}, u32[]{:S(2)}) async-start(bf16[32,16,512]{2,0,1:T(8,128)(2,1)} %bitcast.23), calls=%async_computation.3 | async-start | bytes 1048576 | tf_op jit(solution)/shard_map/all_to_all | solution.py:207
  205.7 12.8 %all-to-all-done.3 = bf16[32,16,512]{2,0,1:T(8,128)(2,1)S(1)} async-done(((bf16[32,16,512]{2,0,1:T(8,128)(2,1)}), bf16[32,16,512]{2,0,1:T(8,128)(2,1)S(1)}, u32[]{:S(2)}, u32[]{:S(2)}) %all-to-all-start.3) | async-done | bytes 524320 | tf_op jit(solution)/shard_map/all_to_all | solution.py:207
  218.5 5.8 %all-to-all-start.4 = ((bf16[32,16,512]{2,0,1:T(8,128)(2,1)}), bf16[32,16,512]{2,0,1:T(8,128)(2,1)}, u32[]{:S(2)}, u32[]{:S(2)}) async-start(bf16[32,16,512]{2,0,1:T(8,128)(2,1)} %bitcast.32), calls=%async_computation.4 | async-start | bytes 1048576 | tf_op jit(solution)/shard_map/all_to_all | solution.py:210
  224.3 19.5 %all-gather.2.cloned.1.call-done = f32[64,4096]{1,0:T(8,128)} async-done(((f32[32,4096]{1,0:T(8,128)}), f32[64,4096]{1,0:T(8,128)}) %all-gather.2.cloned.1.call-update) | async-done | bytes 1048592 | tf_op jit(solution)/shard_map/all_gather | solution.py:214
  243.8 2.3 copy.83
  246.2 7.9 %all-to-all-start.5 = ((f32[64,8,512]{2,0,1:T(8,128)}), f32[64,8,512]{2,0,1:T(8,128)}, u32[]{:S(2)}, u32[]{:S(2)}) async-start(f32[64,8,512]{2,0,1:T(8,128)} %bitcast.250), calls=%async_computation.5 | async-start | bytes 2097152 | tf_op jit(solution)/shard_map/all_to_all | solution.py:215
  254.1 35.7 %psum.14 = f32[512]{0:T(512)S(1)} all-reduce(f32[512]{0:T(512)S(1)} %broadcast_multiply_fusion.1), channel_id=1, replica_groups=mesh['seq'=8,'chan'=16,'dp'=2] {'seq'}, use_global_device_ids=true, to_apply=%region_5.6 | all-reduce | flops 512 | bytes 4096 | tf_op jit(solution)/shard_map/psum | solution.py:12
  289.8 5.5 %psum.15 = f32[512]{0:T(512)} all-reduce(f32[512]{0:T(512)S(1)} %psum.14), channel_id=1, replica_groups=mesh['seq'=8,'chan'=16,'dp'=2] {'dp'}, use_global_device_ids=true, to_apply=%region_6.7 | all-reduce | flops 512 | bytes 4096 | tf_op jit(solution)/shard_map/psum | solution.py:12
  295.3 3.2 %fusion.150 = (bf16[512,512]{0,1:T(8,128)(2,1)}, bf16[512,512]{0,1:T(8,128)(2,1)}, bf16[512,512]{0,1:T(8,128)(2,1)}, bf16[512,512]{0,1:T(8,128)(2,1)}) fusion(bf16[512,512]{0,1:T(8,128)(2,1)S(1)} %copy-done.11, bf16[32,16,512]{2,0,1:T(8,128)(2,1)} %all-to-all-done.4, bf16[1,512,512]{1,2,0:T(8,128)(2,1)S(1)} %copy-done.5, f32[512]{0:T(512)S(1)} %copy-done.20, ...), kind=kLoop, calls=%fused_computation.173 | loop fusion | flops 5242880 | bytes 6293504 | tf_op jit(solution)/shard_map/convert_element_type | solution.py:224
  298.5 2.1 copy.65
  (211 shorter events, 106.2 us)
Async XLA Ops:
  7.2 1.6 copy-start.17
  7.2 1.9 copy-start.18
  8.8 1.7 copy-start.4
  10.5 29.4 %copy-start.15 = (f32[512,512]{1,0:T(8,128)S(1)}, f32[512,512]{1,0:T(8,128)}, u32[]{:S(2)}) copy-start(f32[512,512]{1,0:T(8,128)} %param.12) | copy-start | bytes 3145732
  34.1 20.2 %all-to-all-start = ((bf16[16,32,512]{2,1,0:T(8,128)(2,1)}), bf16[16,32,512]{2,1,0:T(8,128)(2,1)S(1)}, u32[]{:S(2)}, u32[]{:S(2)}) async-start(bf16[16,32,512]{2,1,0:T(8,128)(2,1)} %bitcast.4), calls=%async_computation | async-start | bytes 1048576 | tf_op jit(solution)/shard_map/all_to_all | solution.py:186
  54.4 34.0 %all-to-all-start.2 = ((f32[8,64,512]{2,1,0:T(8,128)}), f32[8,64,512]{2,1,0:T(8,128)S(1)}, u32[]{:S(2)}, u32[]{:S(2)}) async-start(f32[8,64,512]{2,1,0:T(8,128)} %bitcast.18), calls=%async_computation.2 | async-start | bytes 2097152 | tf_op jit(solution)/shard_map/all_to_all | solution.py:182
  106.4 2.5 copy-start.1
  133.4 2.5 copy-start.1
  160.3 2.5 copy-start.1
  187.3 2.5 copy-start.1
  198.6 5.5 %copy-start.19 = (bf16[4,2,8,4096]{3,2,1,0:T(8,128)(2,1)S(1)}, bf16[4,2,8,4096]{3,2,1,0:T(8,128)(2,1)}, u32[]{:S(2)}) copy-start(bf16[4,2,8,4096]{3,2,1,0:T(8,128)(2,1)} %get-tuple-element.118) | copy-start | bytes 1572868
  199.5 19.0 %all-to-all-start.3 = ((bf16[32,16,512]{2,0,1:T(8,128)(2,1)}), bf16[32,16,512]{2,0,1:T(8,128)(2,1)S(1)}, u32[]{:S(2)}, u32[]{:S(2)}) async-start(bf16[32,16,512]{2,0,1:T(8,128)(2,1)} %bitcast.23), calls=%async_computation.3 | async-start | bytes 1048576 | tf_op jit(solution)/shard_map/all_to_all | solution.py:207
  204.0 39.8 %all-gather.2.cloned.1.call-start = ((), (), s32[]{:S(2)}) async-start(), calls=%async_computation.6 | async-start | bytes 1572864 | tf_op jit(solution)/shard_map/all_gather | solution.py:214
  218.5 27.7 %all-to-all-start.4 = ((bf16[32,16,512]{2,0,1:T(8,128)(2,1)}), bf16[32,16,512]{2,0,1:T(8,128)(2,1)}, u32[]{:S(2)}, u32[]{:S(2)}) async-start(bf16[32,16,512]{2,0,1:T(8,128)(2,1)} %bitcast.32), calls=%async_computation.4 | async-start | bytes 1048576 | tf_op jit(solution)/shard_map/all_to_all | solution.py:210
  243.8 51.5 %copy-start.11 = (bf16[512,512]{0,1:T(8,128)(2,1)S(1)}, bf16[512,512]{0,1:T(8,128)(2,1)}, u32[]{:S(2)}) copy-start(bf16[512,512]{0,1:T(8,128)(2,1)} %copy-done.10) | copy-start | bytes 1572868
  246.1 49.1 %copy-start.3 = (bf16[1,512,512]{1,2,0:T(8,128)(2,1)S(1)}, bf16[1,512,512]{1,2,0:T(8,128)(2,1)}, u32[]{:S(2)}) copy-start(bf16[1,512,512]{1,2,0:T(8,128)(2,1)} %copy-done.2) | copy-start | bytes 1572868
  246.1 49.1 %copy-start.5 = (bf16[1,512,512]{1,2,0:T(8,128)(2,1)S(1)}, bf16[1,512,512]{1,2,0:T(8,128)(2,1)}, u32[]{:S(2)}) copy-start(bf16[1,512,512]{1,2,0:T(8,128)(2,1)} %copy-done.4) | copy-start | bytes 1572868
  246.1 49.1 %copy-start.7 = (bf16[1,512,512]{1,2,0:T(8,128)(2,1)S(1)}, bf16[1,512,512]{1,2,0:T(8,128)(2,1)}, u32[]{:S(2)}) copy-start(bf16[1,512,512]{1,2,0:T(8,128)(2,1)} %copy-done.6) | copy-start | bytes 1572868
  246.2 49.1 %copy-start.9 = (bf16[1,512,512]{1,2,0:T(8,128)(2,1)S(1)}, bf16[1,512,512]{1,2,0:T(8,128)(2,1)}, u32[]{:S(2)}) copy-start(bf16[1,512,512]{1,2,0:T(8,128)(2,1)} %copy-done.8) | copy-start | bytes 1572868
  246.2 49.2 %copy-start.20 = (f32[512]{0:T(512)S(1)}, f32[512]{0:T(512)}, u32[]{:S(2)}) copy-start(f32[512]{0:T(512)} %param.13) | copy-start | bytes 6148
  246.2 57.5 %all-to-all-start.5 = ((f32[64,8,512]{2,0,1:T(8,128)}), f32[64,8,512]{2,0,1:T(8,128)}, u32[]{:S(2)}, u32[]{:S(2)}) async-start(f32[64,8,512]{2,0,1:T(8,128)} %bitcast.250), calls=%async_computation.5 | async-start | bytes 2097152 | tf_op jit(solution)/shard_map/all_to_all | solution.py:215
  298.5 2.1 copy-start.14
  298.5 3.1 %copy-start.13 = (bf16[512,512]{0,1:T(8,128)(2,1)S(1)}, bf16[512,512]{0,1:T(8,128)(2,1)}, u32[]{:S(2)}) copy-start(bf16[512,512]{0,1:T(8,128)(2,1)} %get-tuple-element.265) | copy-start | bytes 1572868
  300.7 2.0 copy-start.12
  (9 other events, 11.4 us)
Sparse Core Ops, SparseCore 0:
  206.6 37.1 all-gather.1
